TPU v7x, 256 devices: a whole 4x4x8 slice. The times are simulated.
256 devices in a mesh: dp: 4 (over x), seq: 4 (over y_hi, core), tensor: 16 (over y_lo, z).
Axes of the slice: x: 4, y: 4 (y_hi: 2, y_lo: 2; y = y_hi * 2 + y_lo), z: 8, core: 2. Of those that a mesh axis runs over, the one named last changes fastest.
Arguments:
- byte_acts: bfloat16 [4, 16384, 2048], P('dp', 'seq', 'tensor'), may hold values from -18 to 18
- conv_weight: bfloat16 [16, 1024, 128], P('tensor'), may hold values from -0.1875 to 0.1875
- conv_bias: float32 [2048], P('tensor'), may hold values from -3 to 3
- proj_weight: bfloat16 [2048, 8192], P(None, 'tensor'), may hold values from -0.125 to 0.125
- teacher: bfloat16 [4, 4096, 8192], P('dp', 'seq', 'tensor'), may hold values from -6 to 6
- span_lengths: int32 [4, 4096], P('dp'), may hold values from 1 to 16, as said below
Outputs:
- downsampled: bfloat16 [4, 4096, 2048], P('dp', 'seq', 'tensor')
- byte_grad: bfloat16 [4, 16384, 2048], P('dp', 'seq', 'tensor')
- conv_grad: float32 [16, 1024, 128], P('tensor')
- proj_grad: float32 [2048, 8192], P(None, 'tensor')
Inputs may be any that keep to these rules, and one draw needn't show every extreme that they name: `span_lengths`: each document's 4096 span lengths cover its 16384 bytes in order; the longest is exactly 16.
All inputs are finite; a program needn't handle non-finite values.
Results may differ from a plain program's by a relative error of at most 0.019.
Values may be sent and summed in bfloat16 or wider, within the bound.
No kernel may reach another device: no remote copies, remote signals or barrier semaphores. Data moves between devices by JAX's collectives and lax.ppermute only.
A program may use at most 64 MiB of HBM per device.

v0:
```python
import jax
import jax.numpy as jnp
from jax import lax
from jax.sharding import PartitionSpec as P

STRIDE = 4
KERNEL = 8


def shifted(block, axis, distance):
    devices = range(lax.axis_size(axis))
    route = [(i - distance, i) for i in devices if i - distance in devices]
    return lax.ppermute(block, axis, route)


def intersection_weights(span_start, span_end, span_lengths, first_position, position_count):
    byte_first = (first_position + jnp.arange(position_count, dtype=jnp.int32)) * STRIDE
    lower_edge = jnp.maximum(span_start[:, None], byte_first[None, :])
    upper_edge = jnp.minimum(span_end[:, None], byte_first[None, :] + STRIDE)
    covered = jnp.maximum(upper_edge - lower_edge, 0).astype(jnp.float32)
    return (covered / span_lengths[:, None].astype(jnp.float32)).astype(jnp.bfloat16)


def local(byte_acts, conv_weight, conv_bias, proj_weight, teacher, span_lengths):
    byte_rows = byte_acts[0]
    row_total, width = byte_rows.shape
    groups_here = conv_weight.shape[0]
    group_width = width // groups_here
    positions = row_total // STRIDE
    seq_count = lax.axis_size("seq")
    seq_rank = lax.axis_index("seq")
    lengths_doc = span_lengths[0]
    tokens_all = lengths_doc.shape[0]
    span_end = jnp.cumsum(lengths_doc)
    span_start = span_end - lengths_doc
    next_rows = shifted(byte_rows[:STRIDE], "seq", -1)
    extended = jnp.concatenate([byte_rows, next_rows], axis=0)
    blocks = extended.reshape(positions + 1, STRIDE, groups_here, group_width)
    windows = jnp.concatenate([blocks[:-1], blocks[1:]], axis=1)
    taps_weight = conv_weight.reshape(groups_here, KERNEL, group_width, group_width)
    conv_out = jnp.einsum(
        "pkgc,gkco->pgo", windows, taps_weight, preferred_element_type=jnp.float32
    )
    conv_out = conv_out + conv_bias.reshape(groups_here, group_width)[None]
    downsampled = conv_out.reshape(positions, width).astype(jnp.bfloat16)
    local_weight = intersection_weights(
        span_start, span_end, lengths_doc, seq_rank * positions, positions
    )
    weight_part = local_weight
    pooled_sum = lax.psum_scatter(
        jnp.dot(weight_part, downsampled, preferred_element_type=jnp.float32).astype(jnp.bfloat16),
        "seq",
        scatter_dimension=0,
        tiled=True,
    )
    gathered = lax.all_gather(pooled_sum, "tensor", axis=1, tiled=True)
    predicted = jnp.dot(gathered, proj_weight, preferred_element_type=jnp.float32)
    err_grad = (predicted - teacher[0].astype(jnp.float32)).astype(jnp.bfloat16)
    proj_local = lax.dot_general(
        gathered, err_grad, (((0,), (0,)), ((), ())), preferred_element_type=jnp.float32
    )
    token_scale = 1.0 / jnp.sqrt(jnp.float32(lax.axis_size("dp") * tokens_all))
    proj_summed = lax.psum(proj_local.astype(jnp.bfloat16), ("dp", "seq")).astype(jnp.float32)
    proj_grad = proj_summed * token_scale
    weight_part = proj_weight
    pooled_grad_t = lax.psum_scatter(
        lax.dot_general(
            weight_part, err_grad, (((1,), (1,)), ((), ())), preferred_element_type=jnp.float32
        ).astype(jnp.bfloat16),
        "tensor",
        scatter_dimension=0,
        tiled=True,
    )
    weight_part = local_weight
    down_sum = lax.dot_general(
        weight_part,
        lax.all_gather(pooled_grad_t, "seq", axis=1, tiled=True),
        (((0,), (1,)), ((), ())),
        preferred_element_type=jnp.float32,
    )
    down_grad = down_sum.astype(jnp.bfloat16).reshape(positions, groups_here, group_width)
    conv_local = jnp.einsum(
        "pkgc,pgo->gkco", windows, down_grad, preferred_element_type=jnp.float32
    )
    conv_summed = lax.psum(conv_local.astype(jnp.bfloat16), ("dp", "seq")).astype(jnp.float32)
    position_scale = 1.0 / jnp.sqrt(jnp.float32(lax.axis_size("dp") * positions * seq_count))
    conv_grad = (conv_summed * position_scale).reshape(
        groups_here, KERNEL * group_width, group_width
    )
    window_grad = jnp.einsum(
        "pgo,gkco->pkgc", down_grad, taps_weight, preferred_element_type=jnp.float32
    )
    incoming = shifted(window_grad[-1, STRIDE:], "seq", 1)
    carried_grad = jnp.concatenate([incoming[None], window_grad[:-1, STRIDE:]], axis=0)
    byte_grad = (
        (window_grad[:, :STRIDE] + carried_grad).reshape(row_total, width).astype(jnp.bfloat16)
    )
    return (downsampled[None], byte_grad[None], conv_grad, proj_grad)


def solution(mesh):
    return jax.shard_map(
        local,
        mesh=mesh,
        in_specs=(
            P("dp", "seq", "tensor"),
            P("tensor", None, None),
            P("tensor"),
            P(None, "tensor"),
            P("dp", "seq", "tensor"),
            P("dp", None),
        ),
        out_specs=(
            P("dp", "seq", "tensor"),
            P("dp", "seq", "tensor"),
            P("tensor", None, None),
            P(None, "tensor"),
        ),
        check_vma=False,
    )
```

profile of v0, /device:TPU:1, one launch (start us, length us, event | category | flops | bytes accessed | tf_op | source)
XLA Modules:
  0.0 448.6 jit_solution(9548664783384587583)
XLA Ops:
  7.2 0.0 copy-start
  7.2 0.0 copy-start.6
  7.2 0.0 copy-start.3
  7.2 0.0 reduce-scatter.5.cloned.1.call-start
  7.2 0.8 slice_bitcast_fusion
  8.1 5.1 %collective-permute-start = (bf16[4,128]{1,0:T(4,128)(2,1)S(1)}, bf16[4,128]{1,0:T(4,128)(2,1)S(1)}, u32[]{:S(2)}, u32[]{:S(2)}) collective-permute-start(bf16[4,128]{1,0:T(4,128)(2,1)S(1)} %slice_bitcast_fusion), channel_id=1, source_target_pairs={{16,0},{32,16},{48,32},{17,1},{33,17},{49,33},{18,2},{34,18},{50,3... | collective-permute-start | bytes 3080 | tf_op jit(solution)/shard_map/ppermute | solution.py:13
  13.2 1.0 reduce-window.9
  14.2 0.1 slice.42
  14.3 0.1 reduce-window.12
  14.4 0.1 slice_reduce_fusion
  14.5 0.8 fusion.23
  15.3 0.7 convert_element_type.87
  16.0 1.4 copy.17
  17.4 0.0 collective-permute-done
  17.4 1.5 pad_maximum_fusion
  18.9 0.1 copy.18
  19.0 0.0 copy-start.1
  19.1 1.0 copy-done.1
  20.0 0.0 copy-done.6
  20.0 0.0 copy-done.3
  20.0 0.7 fusion.11
  20.7 0.0 copy-start.7
  20.8 0.7 copy-done.7
  21.5 7.5 %fusion.2 = bf16[4096,128]{1,0:T(8,128)(2,1)} fusion(f32[4096]{0:T(1024)S(1)} %convert_element_type.87, s32[1024]{0:T(1024)S(1)} %add_multiply_fusion, s32[4096]{0:T(1024)S(1)} %get-tuple-element.6, s32[1024]{0:T(1024)S(1)} %broadcast_add_fusion, s32[4096]{0:T(1024)S(1)} %get-tuple-element.7, bf16[1,128,1024]{1,2,0:T(8,128)(2,1)S(1)} %fusion.11), kind=kOutput, calls=%fused_computation.3 | convolution fusion | flops 1103626240 | bytes 1368064 | tf_op jit(solution)/shard_map/dot_general | solution.py:51
  29.0 0.0 reduce-scatter.5.cloned.1.call-update
  29.0 0.0 all-gather.3.cloned.1.call-start
  29.0 38.1 %reduce-scatter.5.cloned.1.call-done = bf16[1024,128]{1,0:T(8,128)(2,1)} async-done(((bf16[4096,128]{1,0:T(8,128)(2,1)}), bf16[1024,128]{1,0:T(8,128)(2,1)}) %reduce-scatter.5.cloned.1.call-update) | async-done | bytes 262160 | tf_op jit(solution)/shard_map/reduce_scatter | solution.py:50
  67.2 0.0 all-gather.3.cloned.1.call-update
  67.2 0.0 reduce-scatter.7.cloned.1.call-start
  67.2 80.8 %all-gather.3.cloned.1.call-done = bf16[1024,2048]{1,0:T(8,128)(2,1)} async-done(((bf16[1024,128]{1,0:T(8,128)(2,1)}), bf16[1024,2048]{1,0:T(8,128)(2,1)}) %all-gather.3.cloned.1.call-update) | async-done | bytes 4194320 | tf_op jit(solution)/shard_map/all_gather | solution.py:56
  148.1 0.0 copy-done
  148.1 0.0 copy-start.5
  148.1 4.6 %fusion.24 = f32[1024,512]{1,0:T(8,128)S(1)} fusion(bf16[1024,2048]{1,0:T(8,128)(2,1)} %all-gather.3.cloned.1.call-done, bf16[2048,512]{1,0:T(8,128)(2,1)S(1)} %copy-done), kind=kOutput, calls=%fused_computation.37 | convolution fusion | flops 2147483648 | bytes 8388608 | tf_op jit(solution)/shard_map/dot_general | solution.py:57
  152.7 0.0 copy-start.8
  152.7 1.4 copy-done.8
  154.0 0.0 copy-done.5
  154.0 4.4 convert_bitcast_fusion
  158.4 6.4 %copy.23 = bf16[2048,1024]{1,0:T(8,128)(2,1)} copy(bf16[2048,1024]{0,1:T(8,128)(2,1)} %convert_bitcast_fusion) | data formatting | bytes 8388608
  164.9 0.0 reduce-scatter.7.cloned.1.call-update
  164.9 0.0 all-gather.5.cloned.1.call-start
  164.9 78.6 %reduce-scatter.7.cloned.1.call-done = bf16[128,1024]{1,0:T(8,128)(2,1)} async-done(((bf16[2048,1024]{1,0:T(8,128)(2,1)}), bf16[128,1024]{1,0:T(8,128)(2,1)}) %reduce-scatter.7.cloned.1.call-update) | async-done | bytes 262160
  243.5 1.8 copy.24
  245.3 0.0 all-gather.5.cloned.1.call-update
  245.3 0.2 all-reduce.3.cloned.1.call-start
  245.6 6.8 %convolution_convert_fusion = bf16[2048,512]{1,0:T(8,128)(2,1)} fusion(bf16[1024,2048]{1,0:T(8,128)(2,1)} %all-gather.3.cloned.1.call-done, f32[1024,512]{1,0:T(8,128)} %copy-done.8, bf16[1,1024,512]{2,1,0:T(8,128)(2,1)} %param.10), kind=kOutput, calls=%fused_computation.6 | convolution fusion | flops 2150105088 | bytes 9437184 | tf_op jit(solution)/shard_map/dot_general | solution.py:59
  252.3 24.2 %all-gather.5.cloned.1.call-done = bf16[128,4096]{0,1:T(8,128)(2,1)} async-done(((bf16[128,1024]{0,1:T(8,128)(2,1)}), bf16[128,4096]{0,1:T(8,128)(2,1)}) %all-gather.5.cloned.1.call-update) | async-done | bytes 1048592 | tf_op jit(solution)/shard_map/all_gather | solution.py:77
  276.5 0.0 copy-start.2
  276.5 7.7 %fusion.15 = bf16[1024,128,1]{1,0,2:T(8,128)(2,1)S(1)} fusion(bf16[128,4096]{0,1:T(8,128)(2,1)} %all-gather.5.cloned.1.call-done, f32[4096]{0:T(1024)S(1)} %convert_element_type.87, s32[1024]{0:T(1024)S(1)} %add_multiply_fusion, s32[4096]{0:T(1024)S(1)} %get-tuple-element.6, s32[1024]{0:T(1024)S(1)} %broadcast_add_fusion, s32[4096]{0:T(1024)S(1)} %get-tuple-element.7), kind=kOutput, calls=%fused_computation.21 | convolution fusion | flops 1103233024 | bytes 1368064 | tf_op jit(solution)/shard_map/dot_general | solution.py:75
  284.2 0.0 copy-start.4
  284.2 0.7 copy-done.4
  284.9 0.0 copy-done.2
  284.9 1.4 fusion.14
  286.3 0.0 all-reduce.3.cloned.1.call-update
  286.4 1.7 convolution_bitcast_fusion
  288.1 2.1 collective-permute-start.1
  290.1 0.1 slice.46
  290.3 0.8 collective-permute-done.1
  291.1 0.3 fusion.3
  291.4 1.8 copy.20
  293.2 142.9 %all-reduce.3.cloned.1.call-done = (bf16[1,8,128,128]{3,2,1,0:T(8,128)(2,1)}, bf16[2048,512]{1,0:T(8,128)(2,1)}) async-done(((bf16[1,8,128,128]{3,2,1,0:T(8,128)(2,1)}, bf16[2048,512]{1,0:T(8,128)(2,1)}), (bf16[1,8,128,128]{3,2,1,0:T(8,128)(2,1)}, bf16[2048,512]{1,0:T(8,128)(2,1)})) %all-reduce.3.cloned.1.call-update) | async-done | bytes 2359312 | tf_op jit(solution)/shard_map/psum | solution.py:85
  436.1 1.8 convert_multiply_fusion.1
  437.9 4.2 convert_multiply_fusion
  (3 shorter events, 0.0 us)
Async XLA Ops:
  7.2 140.9 %copy-start = (bf16[2048,512]{1,0:T(8,128)(2,1)S(1)}, bf16[2048,512]{1,0:T(8,128)(2,1)}, u32[]{:S(2)}) copy-start(bf16[2048,512]{1,0:T(8,128)(2,1)} %param.9) | copy-start | bytes 6291460
  7.2 12.8 %copy-start.6 = (f32[128]{0:T(128)S(1)}, f32[128]{0:T(128)}, u32[]{:S(2)}) copy-start(f32[128]{0:T(128)} %param.8) | copy-start | bytes 1540
  7.2 12.8 %copy-start.3 = (bf16[1,1024,128]{2,1,0:T(8,128)(2,1)S(1)}, bf16[1,1024,128]{2,1,0:T(8,128)(2,1)}, u32[]{:S(2)}) copy-start(bf16[1,1024,128]{2,1,0:T(8,128)(2,1)} %param.7) | copy-start | bytes 786436
  7.2 60.0 %reduce-scatter.5.cloned.1.call-start = ((), (), s32[]{:S(2)}) async-start(), calls=%async_computation.2 | async-start | bytes 1310720 | tf_op jit(solution)/shard_map/reduce_scatter | solution.py:50
  8.1 9.3 %collective-permute-start = (bf16[4,128]{1,0:T(4,128)(2,1)S(1)}, bf16[4,128]{1,0:T(4,128)(2,1)S(1)}, u32[]{:S(2)}, u32[]{:S(2)}) collective-permute-start(bf16[4,128]{1,0:T(4,128)(2,1)S(1)} %slice_bitcast_fusion), channel_id=1, source_target_pairs={{16,0},{32,16},{48,32},{17,1},{33,17},{49,33},{18,2},{34,18},{50,3... | collective-permute-start | bytes 3080 | tf_op jit(solution)/shard_map/ppermute | solution.py:13
  19.0 1.0 copy-start.1
  20.7 0.7 copy-start.7
  29.0 119.1 %all-gather.3.cloned.1.call-start = ((), (), s32[]{:S(2)}) async-start(), calls=%async_computation.3 | async-start | bytes 4456448 | tf_op jit(solution)/shard_map/all_gather | solution.py:56
  67.2 176.3 %reduce-scatter.7.cloned.1.call-start = ((), (), s32[]{:S(2)}) async-start(), calls=%async_computation.5 | async-start | bytes 4456448
  148.1 6.0 %copy-start.5 = (bf16[1,1024,512]{2,1,0:T(8,128)(2,1)S(1)}, bf16[1,1024,512]{2,1,0:T(8,128)(2,1)}, u32[]{:S(2)}) copy-start(bf16[1,1024,512]{2,1,0:T(8,128)(2,1)} %param.10) | copy-start | bytes 3145732
  152.7 1.4 copy-start.8
  164.9 111.6 %all-gather.5.cloned.1.call-start = ((), (), s32[]{:S(2)}) async-start(), calls=%async_computation.4 | async-start | bytes 1310720 | tf_op jit(solution)/shard_map/all_gather | solution.py:77
  245.3 190.8 %all-reduce.3.cloned.1.call-start = ((), (), s32[]{:S(2)}) async-start(), calls=%async_computation.6 | async-start | bytes 4718592 | tf_op jit(solution)/shard_map/psum | solution.py:85
  276.5 8.4 %copy-start.2 = (bf16[1024,4,1,128]{3,0,1,2:T(8,128)(2,1)S(1)}, bf16[1024,4,1,128]{3,0,1,2:T(8,128)(2,1)}, u32[]{:S(2)}) copy-start(bf16[1024,4,1,128]{3,0,1,2:T(8,128)(2,1)} %copy-done.1) | copy-start | bytes 3145732
  284.2 0.7 copy-start.4
  288.1 3.1 collective-permute-start.1
Sparse Core Ops, SparseCore 0:
  29.1 38.0 reduce-scatter.4
  69.0 79.0 all-gather.2
  165.0 78.4 reduce-scatter.6
  245.9 30.5 all-gather.4
  286.5 149.5 all-reduce.2
where the time goes:
time: 449 us
  waiting for transfers between devices  366 us (82%)
  matrix products  34.8 us (8%)
  local copies, waits for them, and re-layouts  16.4 us (4%)
  between operations  13.9 us (3%)
  other arithmetic  10.3 us (2%)
  starting transfers between devices  7.58 us (2%)
    psum x1, waiting for transfers between devices, local(): lax.psum(conv_local.astype(jnp.bfloat16), ('dp', 'seq')).astype(jnp.float32)  143 us
    all_gather x1, waiting for transfers between devices, local(): gathered = lax.all_gather(pooled_sum, 'tensor', axis=1, tiled=True)  80.8 us
    unnamed x6, waiting for transfers between devices  78.7 us
    reduce_scatter x1, waiting for transfers between devices, local(): lax.psum_scatter(jnp.dot(weight_part, downsampled, preferred_element_type...  38.1 us
    all_gather x1, waiting for transfers between devices, local(): lax.all_gather(pooled_grad_t, 'seq', axis=1, tiled=True)  24.2 us
    unnamed x20, local copies, waits for them, and re-layouts  12 us
  transfers between devices with their start and end apart: 7, of which 6 were waited for; matrix products, arithmetic and copies ran while one was open for 3% of the time, Pallas kernels for 0%

commit v1 on v0

--- a/solution.py
+++ b/solution.py
@@ -11,6 +11,39 @@
     devices = range(lax.axis_size(axis))
     route = [(i - distance, i) for i in devices if i - distance in devices]
     return lax.ppermute(block, axis, route)
+
+
+def shard_sum(block, axis):
+    count = lax.axis_size(axis)
+    rank = lax.axis_index(axis)
+    pieces = block.reshape((count, block.shape[0] // count) + block.shape[1:])
+    total = lax.dynamic_index_in_dim(pieces, rank, 0, keepdims=False).astype(jnp.float32)
+    for distance in range(1, count):
+        route = [(i, (i + distance) % count) for i in range(count)]
+        outgoing = lax.dynamic_index_in_dim(pieces, (rank + distance) % count, 0, keepdims=False)
+        total = total + lax.ppermute(outgoing, axis, route).astype(jnp.float32)
+    return total
+
+
+def shard_gather(piece, axis):
+    count = lax.axis_size(axis)
+    rank = lax.axis_index(axis)
+    received = [piece]
+    for distance in range(1, count):
+        route = [(i, (i + distance) % count) for i in range(count)]
+        received.append(lax.ppermute(piece, axis, route))
+    stacked = jnp.stack(received[::-1])
+    ordered = jnp.roll(stacked, rank + 1, axis=0)
+    return ordered.reshape((count * piece.shape[0],) + piece.shape[1:])
+
+
+def permute_psum(block, axes):
+    summed = block
+    for axis in axes:
+        summed = shard_sum(summed, axis).astype(block.dtype)
+    for axis in axes[::-1]:
+        summed = shard_gather(summed, axis)
+    return summed
 
 
 def intersection_weights(span_start, span_end, span_lengths, first_position, position_count):
@@ -46,12 +79,14 @@
     local_weight = intersection_weights(
         span_start, span_end, lengths_doc, seq_rank * positions, positions
     )
-    weight_part = local_weight
-    pooled_sum = lax.psum_scatter(
-        jnp.dot(weight_part, downsampled, preferred_element_type=jnp.float32).astype(jnp.bfloat16),
-        "seq",
-        scatter_dimension=0,
-        tiled=True,
+    tokens_here = tokens_all // seq_count
+    own_start = lax.dynamic_slice_in_dim(span_start, seq_rank * tokens_here, tokens_here)
+    own_end = lax.dynamic_slice_in_dim(span_end, seq_rank * tokens_here, tokens_here)
+    own_lengths = lax.dynamic_slice_in_dim(lengths_doc, seq_rank * tokens_here, tokens_here)
+    token_weight = intersection_weights(own_start, own_end, own_lengths, 0, positions * seq_count)
+    down_all = lax.all_gather(downsampled, "seq", axis=0, tiled=True)
+    pooled_sum = jnp.dot(token_weight, down_all, preferred_element_type=jnp.float32).astype(
+        jnp.bfloat16
     )
     gathered = lax.all_gather(pooled_sum, "tensor", axis=1, tiled=True)
     predicted = jnp.dot(gathered, proj_weight, preferred_element_type=jnp.float32)
@@ -60,7 +95,7 @@
         gathered, err_grad, (((0,), (0,)), ((), ())), preferred_element_type=jnp.float32
     )
     token_scale = 1.0 / jnp.sqrt(jnp.float32(lax.axis_size("dp") * tokens_all))
-    proj_summed = lax.psum(proj_local.astype(jnp.bfloat16), ("dp", "seq")).astype(jnp.float32)
+    proj_summed = permute_psum(proj_local.astype(jnp.bfloat16), ("dp", "seq")).astype(jnp.float32)
     proj_grad = proj_summed * token_scale
     weight_part = proj_weight
     pooled_grad_t = lax.psum_scatter(

time: 449 us -> 446 us (level)
  waiting for transfers between devices: 366 us -> 317 us
  starting transfers between devices: 7.58 us -> 35.4 us
  local copies, waits for them, and re-layouts: 16.4 us -> 33.3 us
    unnamed x6, waiting for transfers between devices: 78.7 us -> 0.08 us
    ppermute x0 -> x12, waiting for transfers between devices: none -> 68.1 us  [the longest x6 36.7 us: shard_gather(): received.append(lax.ppermute(piece, axis, route))]
    reduce_scatter x1 -> x0, waiting for transfers between devices: 38.1 us -> none  [local(): lax.psum_scatter(jnp.dot(weight_part, downsampled, preferred_element_type...]
    ppermute x0 -> x12, starting transfers between devices: none -> 27.8 us  [the longest x6 18.2 us: shard_sum(): total = total + lax.ppermute(outgoing, axis, route).astype(jnp.float32)]
    all_gather x0 -> x1, waiting for transfers between devices: none -> 23.7 us  [local(): down_all = lax.all_gather(downsampled, 'seq', axis=0, tiled=True)]
    all_gather x1, waiting for transfers between devices: 24.2 us -> 7.43 us  [local(): lax.all_gather(pooled_grad_t, 'seq', axis=1, tiled=True)]
    unnamed x20 -> x48, local copies, waits for them, and re-layouts: 12 us -> 24 us
    psum x1, waiting for transfers between devices: 143 us -> 138 us  [local(): lax.psum(conv_local.astype(jnp.bfloat16), ('dp', 'seq')).astype(jnp.float32)]
  transfers between devices with their start and end apart: 7 -> 19, of which waited for: 6 -> 15; matrix products, arithmetic and copies ran while one was open for 3% -> 8% of each run, Pallas kernels for 0% -> 0%
where the time goes in v1:
time: 446 us
  waiting for transfers between devices  317 us (71%)
  starting transfers between devices  35.4 us (8%)
  local copies, waits for them, and re-layouts  33.3 us (7%)
  matrix products  32.8 us (7%)
  between operations  14.2 us (3%)
  other arithmetic  13.4 us (3%)
    psum x1, waiting for transfers between devices, local(): lax.psum(conv_local.astype(jnp.bfloat16), ('dp', 'seq')).astype(jnp.float32)  138 us
    all_gather x1, waiting for transfers between devices, local(): gathered = lax.all_gather(pooled_sum, 'tensor', axis=1, tiled=True)  78.7 us
    ppermute x6, waiting for transfers between devices, shard_gather(): received.append(lax.ppermute(piece, axis, route))  36.7 us
    ppermute x6, waiting for transfers between devices, shard_sum(): total = total + lax.ppermute(outgoing, axis, route).astype(jnp.float32)  31.5 us
    unnamed x48, local copies, waits for them, and re-layouts  24 us
    all_gather x1, waiting for transfers between devices, local(): down_all = lax.all_gather(downsampled, 'seq', axis=0, tiled=True)  23.7 us
    ppermute x6, starting transfers between devices, shard_sum(): total = total + lax.ppermute(outgoing, axis, route).astype(jnp.float32)  18.2 us
    ppermute x6, starting transfers between devices, shard_gather(): received.append(lax.ppermute(piece, axis, route))  9.53 us
  transfers between devices with their start and end apart: 19, of which 15 were waited for; matrix products, arithmetic and copies ran while one was open for 8% of the time, Pallas kernels for 0%

profile of v1, /device:TPU:1, one launch (start us, length us, event | category | flops | bytes accessed | tf_op | source)
XLA Modules:
  0.0 445.7 jit_solution(11971532625960414713)
XLA Ops:
  7.2 0.8 slice_bitcast_fusion
  8.1 5.1 %collective-permute-start = (bf16[4,128]{1,0:T(4,128)(2,1)S(1)}, bf16[4,128]{1,0:T(4,128)(2,1)S(1)}, u32[]{:S(2)}, u32[]{:S(2)}) collective-permute-start(bf16[4,128]{1,0:T(4,128)(2,1)S(1)} %slice_bitcast_fusion), channel_id=1, source_target_pairs={{16,0},{32,16},{48,32},{17,1},{33,17},{49,33},{18,2},{34,18},{50,3... | collective-permute-start | bytes 3080 | tf_op jit(solution)/shard_map/ppermute | solution.py:13
  13.2 1.4 copy.17
  14.6 0.9 collective-permute-done
  15.5 1.5 pad_maximum_fusion
  17.0 0.1 copy.18
  17.2 1.0 copy-done.5
  18.2 1.4 fusion.10
  19.7 0.3 reduce-window.9
  20.4 23.7 %all-gather.9.cloned.1.call-done = bf16[4096,1,128]{2,0,1:T(8,128)(2,1)} async-done(((bf16[1024,1,128]{2,0,1:T(8,128)(2,1)}), bf16[4096,1,128]{2,0,1:T(8,128)(2,1)}) %all-gather.9.cloned.1.call-update) | async-done | bytes 1048592 | tf_op jit(solution)/shard_map/all_gather | solution.py:87
  44.1 7.4 %fusion.13 = bf16[1024,128]{1,0:T(8,128)(2,1)} fusion(f32[1024]{0:T(1024)S(1)} %bitcast.150, s32[4096]{0:T(1024)S(1)} %get-tuple-element.14, s32[1024]{0:T(1024)S(1)} %dynamic_slice.44, s32[4096]{0:T(1024)S(1)} %get-tuple-element.15, s32[1024]{0:T(1024)S(1)} %dynamic_slice.43, bf16[4096,1,128]{2,0,1:T(8,128)(2,1)} %all-gather.9.cloned.1.call-done), kind=kOutput, calls=%fused_computation.20 | convolution fusion | flops 1103233024 | bytes 1355776 | tf_op jit(solution)/shard_map/dot_general | solution.py:88
  51.6 78.7 %all-gather.5.cloned.1.call-done = bf16[1024,2048]{1,0:T(8,128)(2,1)} async-done(((bf16[1024,128]{1,0:T(8,128)(2,1)}), bf16[1024,2048]{1,0:T(8,128)(2,1)}) %all-gather.5.cloned.1.call-update) | async-done | bytes 4194320 | tf_op jit(solution)/shard_map/all_gather | solution.py:91
  130.4 4.5 %fusion.30 = f32[1024,512]{1,0:T(8,128)S(1)} fusion(bf16[1024,2048]{1,0:T(8,128)(2,1)} %all-gather.5.cloned.1.call-done, bf16[2048,512]{1,0:T(8,128)(2,1)S(1)} %copy-done), kind=kOutput, calls=%fused_computation.72 | convolution fusion | flops 2147483648 | bytes 8388608 | tf_op jit(solution)/shard_map/dot_general | solution.py:92
  134.9 1.4 copy-done.15
  136.3 4.4 convert_bitcast_fusion
  140.7 6.4 %copy.23 = bf16[2048,1024]{1,0:T(8,128)(2,1)} copy(bf16[2048,1024]{0,1:T(8,128)(2,1)} %convert_bitcast_fusion) | data formatting | bytes 8388608
  147.2 5.3 %convolution_convert_fusion = bf16[2048,512]{1,0:T(8,128)(2,1)S(1)} fusion(bf16[1024,2048]{1,0:T(8,128)(2,1)} %all-gather.5.cloned.1.call-done, f32[1024,512]{1,0:T(8,128)} %copy-done.15, bf16[1,1024,512]{2,1,0:T(8,128)(2,1)S(1)} %copy-done.13), kind=kOutput, calls=%fused_computation.6 | convolution fusion | flops 2150105088 | bytes 9437184 | tf_op jit(solution)/shard_map/dot_general | solution.py:94
  152.5 1.3 copy-done.2
  153.8 0.9 dynamic-slice_bitcast_fusion.2
  154.7 1.2 collective-permute-start.2
  155.8 1.5 collective-permute-start.4
  157.3 1.5 collective-permute-start.3
  158.8 5.4 %collective-permute-done.2 = bf16[512,512]{1,0:T(8,128)(2,1)} collective-permute-done((bf16[512,512]{1,0:T(8,128)(2,1)}, bf16[512,512]{1,0:T(8,128)(2,1)}, u32[]{:S(2)}, u32[]{:S(2)}) %collective-permute-start.2) | collective-permute-done | bytes 524320 | tf_op jit(solution)/shard_map/ppermute | solution.py:24
  164.2 4.3 collective-permute-done.4
  168.5 3.1 collective-permute-done.3
  171.7 1.8 fusion.18
  173.5 13.9 %collective-permute-start.5 = (bf16[128,512]{1,0:T(8,128)(2,1)S(1)}, bf16[128,512]{1,0:T(8,128)(2,1)S(1)}, u32[]{:S(2)}, u32[]{:S(2)}) collective-permute-start(bf16[128,512]{1,0:T(8,128)(2,1)S(1)} %get-tuple-element.9), channel_id=1, source_target_pairs={{0,16},{16,32},{32,48},{48,0},{1,17},{17,33},{33,49},{49,1},{2,18}... | collective-permute-start | bytes 393224 | tf_op jit(solution)/shard_map/ppermute | solution.py:24
  187.4 0.2 collective-permute-start.6
  187.6 9.2 %collective-permute-done.5 = bf16[128,512]{1,0:T(8,128)(2,1)S(1)} collective-permute-done((bf16[128,512]{1,0:T(8,128)(2,1)S(1)}, bf16[128,512]{1,0:T(8,128)(2,1)S(1)}, u32[]{:S(2)}, u32[]{:S(2)}) %collective-permute-start.5) | collective-permute-done | bytes 131104 | tf_op jit(solution)/shard_map/ppermute | solution.py:24
  196.7 6.4 %collective-permute-done.7 = bf16[128,512]{1,0:T(8,128)(2,1)S(1)} collective-permute-done((bf16[128,512]{1,0:T(8,128)(2,1)S(1)}, bf16[128,512]{1,0:T(8,128)(2,1)S(1)}, u32[]{:S(2)}, u32[]{:S(2)}) %collective-permute-start.7) | collective-permute-done | bytes 131104 | tf_op jit(solution)/shard_map/ppermute | solution.py:24
  203.1 3.1 collective-permute-done.6
  206.2 1.0 fusion.24
  207.2 1.8 collective-permute-start.8
  209.0 3.9 collective-permute-start.10
  212.9 1.9 collective-permute-start.9
  214.8 7.5 %collective-permute-done.8 = bf16[128,512]{1,0:T(8,128)(2,1)S(1)} collective-permute-done((bf16[128,512]{1,0:T(8,128)(2,1)S(1)}, bf16[128,512]{1,0:T(8,128)(2,1)S(1)}, u32[]{:S(2)}, u32[]{:S(2)}) %collective-permute-start.8) | collective-permute-done | bytes 131104 | tf_op jit(solution)/shard_map/ppermute | solution.py:34
  222.3 7.9 %collective-permute-done.9 = bf16[128,512]{1,0:T(8,128)(2,1)S(1)} collective-permute-done((bf16[128,512]{1,0:T(8,128)(2,1)S(1)}, bf16[128,512]{1,0:T(8,128)(2,1)S(1)}, u32[]{:S(2)}, u32[]{:S(2)}) %collective-permute-start.9) | collective-permute-done | bytes 131104 | tf_op jit(solution)/shard_map/ppermute | solution.py:34
  230.4 1.2 collective-permute-start.11
  231.7 0.5 collective-permute-start.12
  232.2 0.2 collective-permute-start.13
  232.4 12.0 %collective-permute-done.11 = bf16[512,512]{1,0:T(8,128)(2,1)S(1)} collective-permute-done((bf16[512,512]{1,0:T(8,128)(2,1)S(1)}, bf16[512,512]{1,0:T(8,128)(2,1)S(1)}, u32[]{:S(2)}, u32[]{:S(2)}) %collective-permute-start.11) | collective-permute-done | bytes 524320 | tf_op jit(solution)/shard_map/ppermute | solution.py:34
  244.4 0.9 bitcast_dynamic-update-slice_fusion.6
  245.3 1.8 copy.24
  247.1 0.3 all-reduce.2.cloned.1.call-start
  247.4 1.9 bitcast_dynamic-update-slice_fusion.4
  249.2 9.2 %collective-permute-done.13 = bf16[512,512]{1,0:T(8,128)(2,1)} collective-permute-done((bf16[512,512]{1,0:T(8,128)(2,1)S(1)}, bf16[512,512]{1,0:T(8,128)(2,1)}, u32[]{:S(2)}, u32[]{:S(2)}) %collective-permute-start.13) | collective-permute-done | bytes 524320 | tf_op jit(solution)/shard_map/ppermute | solution.py:34
  258.4 1.9 bitcast_dynamic-update-slice_fusion.2
  260.3 0.8 bitcast_dynamic-update-slice_fusion
  261.1 0.8 bitcast_dynamic-update-slice_fusion.7
  262.0 1.9 bitcast_dynamic-update-slice_fusion.5
  263.8 1.9 bitcast_dynamic-update-slice_fusion.3
  265.8 0.9 bitcast_dynamic-update-slice_fusion.1
  266.6 4.4 convert_multiply_fusion
  271.0 7.4 %all-gather.7.cloned.1.call-done = bf16[128,4096]{0,1:T(8,128)(2,1)} async-done(((bf16[128,1024]{0,1:T(8,128)(2,1)}), bf16[128,4096]{0,1:T(8,128)(2,1)}) %all-gather.7.cloned.1.call-update) | async-done | bytes 1048592 | tf_op jit(solution)/shard_map/all_gather | solution.py:112
  278.4 7.6 %fusion.15 = bf16[1024,128,1]{1,0,2:T(8,128)(2,1)S(1)} fusion(bf16[128,4096]{0,1:T(8,128)(2,1)} %all-gather.7.cloned.1.call-done, f32[4096]{0:T(1024)S(1)} %convert_element_type.141, s32[1024]{0:T(1024)S(1)} %get-tuple-element.12, s32[4096]{0:T(1024)S(1)} %copy-done.10, s32[1024]{0:T(1024)S(1)} %get-tuple-element.13, s32[4096]{0:T(1024)S(1)} %copy-done.12), kind=kOutput, calls=%fused_computation.22 | convolution fusion | flops 1103233024 | bytes 1368064 | tf_op jit(solution)/shard_map/dot_general | solution.py:110
  286.0 0.7 convolution_bitcast_fusion
  286.8 2.0 copy-done.1
  288.7 2.1 collective-permute-start.1
  290.8 1.5 fusion.14
  292.3 3.1 slice.46
  295.4 2.5 fusion.2
  297.9 1.8 copy.20
  299.7 137.7 %all-reduce.2.cloned.1.call-done = bf16[1,8,128,128]{3,2,1,0:T(8,128)(2,1)} async-done(((bf16[1,8,128,128]{3,2,1,0:T(8,128)(2,1)}), bf16[1,8,128,128]{3,2,1,0:T(8,128)(2,1)}) %all-reduce.2.cloned.1.call-update) | async-done | bytes 262160 | tf_op jit(solution)/shard_map/psum | solution.py:120
  437.4 1.8 convert_multiply_fusion.1
  (63 shorter events, 0.9 us)
Async XLA Ops:
  7.2 123.2 %copy-start = (bf16[2048,512]{1,0:T(8,128)(2,1)S(1)}, bf16[2048,512]{1,0:T(8,128)(2,1)}, u32[]{:S(2)}) copy-start(bf16[2048,512]{1,0:T(8,128)(2,1)} %param.9) | copy-start | bytes 6291460
  7.2 11.0 %copy-start.14 = (f32[128]{0:T(128)S(1)}, f32[128]{0:T(128)}, u32[]{:S(2)}) copy-start(f32[128]{0:T(128)} %param.8) | copy-start | bytes 1540
  7.2 11.0 %copy-start.7 = (bf16[1,1024,128]{2,1,0:T(8,128)(2,1)S(1)}, bf16[1,1024,128]{2,1,0:T(8,128)(2,1)}, u32[]{:S(2)}) copy-start(bf16[1,1024,128]{2,1,0:T(8,128)(2,1)} %param.7) | copy-start | bytes 786436
  7.2 36.9 %all-gather.9.cloned.1.call-start = ((), (), s32[]{:S(2)}) async-start(), calls=%async_computation.4 | async-start | bytes 1310720 | tf_op jit(solution)/shard_map/all_gather | solution.py:87
  8.1 7.4 %collective-permute-start = (bf16[4,128]{1,0:T(4,128)(2,1)S(1)}, bf16[4,128]{1,0:T(4,128)(2,1)S(1)}, u32[]{:S(2)}, u32[]{:S(2)}) collective-permute-start(bf16[4,128]{1,0:T(4,128)(2,1)S(1)} %slice_bitcast_fusion), channel_id=1, source_target_pairs={{16,0},{32,16},{48,32},{17,1},{33,17},{49,33},{18,2},{34,18},{50,3... | collective-permute-start | bytes 3080 | tf_op jit(solution)/shard_map/ppermute | solution.py:13
  14.6 5.0 %copy-start.3 = (bf16[1024,4,1,128]{3,0,1,2:T(8,128)(2,1)}, bf16[1024,4,1,128]{3,0,1,2:T(8,128)(2,1)S(1)}, u32[]{:S(2)}) copy-start(bf16[1024,4,1,128]{3,0,1,2:T(8,128)(2,1)S(1)} %copy.17) | copy-start | bytes 3145732
  15.5 4.2 copy-start.8
  17.2 1.0 copy-start.5
  19.6 110.7 %all-gather.5.cloned.1.call-start = ((), (), s32[]{:S(2)}) async-start(), calls=%async_computation.1 | async-start | bytes 4456448 | tf_op jit(solution)/shard_map/all_gather | solution.py:91
  20.3 31.3 %copy-start.9 = (s32[4096]{0:T(1024)}, s32[4096]{0:T(1024)S(1)}, u32[]{:S(2)}) copy-start(s32[4096]{0:T(1024)S(1)} %get-tuple-element.4) | copy-start | bytes 49156
  20.3 31.3 %copy-start.11 = (s32[4096]{0:T(1024)}, s32[4096]{0:T(1024)S(1)}, u32[]{:S(2)}) copy-start(s32[4096]{0:T(1024)S(1)} %get-tuple-element.5) | copy-start | bytes 49156
  51.6 84.7 %copy-start.13 = (bf16[1,1024,512]{2,1,0:T(8,128)(2,1)S(1)}, bf16[1,1024,512]{2,1,0:T(8,128)(2,1)}, u32[]{:S(2)}) copy-start(bf16[1,1024,512]{2,1,0:T(8,128)(2,1)} %param.10) | copy-start | bytes 3145732
  51.6 193.7 %reduce-scatter.4.cloned.1.call-start = ((), (), s32[]{:S(2)}) async-start(), calls=%async_computation.5 | async-start | bytes 4456448
  134.9 1.4 copy-start.15
  147.1 131.3 %all-gather.7.cloned.1.call-start = ((), (), s32[]{:S(2)}) async-start(), calls=%async_computation.2 | async-start | bytes 1310720 | tf_op jit(solution)/shard_map/all_gather | solution.py:112
  152.4 1.3 copy-start.2
  154.7 9.6 %collective-permute-start.2 = (bf16[512,512]{1,0:T(8,128)(2,1)}, bf16[512,512]{1,0:T(8,128)(2,1)}, u32[]{:S(2)}, u32[]{:S(2)}) collective-permute-start(bf16[512,512]{1,0:T(8,128)(2,1)} %get-tuple-element.6), channel_id=1, source_target_pairs={{0,64},{64,128},{128,192},{192,0},{1,65},{65,129},{129,193},{193,1... | collective-permute-start | bytes 1572872 | tf_op jit(solution)/shard_map/ppermute | solution.py:24
  155.8 12.7 %collective-permute-start.4 = (bf16[512,512]{1,0:T(8,128)(2,1)S(1)}, bf16[512,512]{1,0:T(8,128)(2,1)}, u32[]{:S(2)}, u32[]{:S(2)}) collective-permute-start(bf16[512,512]{1,0:T(8,128)(2,1)S(1)} %get-tuple-element.7), channel_id=1, source_target_pairs={{0,192},{64,0},{128,64},{192,128},{1,193},{65,1},{129,65},{193,129... | collective-permute-start | bytes 1572872 | tf_op jit(solution)/shard_map/ppermute | solution.py:24
  157.3 14.3 %collective-permute-start.3 = (bf16[512,512]{1,0:T(8,128)(2,1)S(1)}, bf16[512,512]{1,0:T(8,128)(2,1)}, u32[]{:S(2)}, u32[]{:S(2)}) collective-permute-start(bf16[512,512]{1,0:T(8,128)(2,1)S(1)} %get-tuple-element.8), channel_id=1, source_target_pairs={{0,128},{64,192},{128,0},{192,64},{1,129},{65,193},{129,1},{193,65... | collective-permute-start | bytes 1572872 | tf_op jit(solution)/shard_map/ppermute | solution.py:24
  173.5 23.2 %collective-permute-start.5 = (bf16[128,512]{1,0:T(8,128)(2,1)S(1)}, bf16[128,512]{1,0:T(8,128)(2,1)S(1)}, u32[]{:S(2)}, u32[]{:S(2)}) collective-permute-start(bf16[128,512]{1,0:T(8,128)(2,1)S(1)} %get-tuple-element.9), channel_id=1, source_target_pairs={{0,16},{16,32},{32,48},{48,0},{1,17},{17,33},{33,49},{49,1},{2,18}... | collective-permute-start | bytes 393224 | tf_op jit(solution)/shard_map/ppermute | solution.py:24
  187.4 15.8 %collective-permute-start.7 = (bf16[128,512]{1,0:T(8,128)(2,1)S(1)}, bf16[128,512]{1,0:T(8,128)(2,1)S(1)}, u32[]{:S(2)}, u32[]{:S(2)}) collective-permute-start(bf16[128,512]{1,0:T(8,128)(2,1)S(1)} %get-tuple-element.10), channel_id=1, source_target_pairs={{0,48},{16,0},{32,16},{48,32},{1,49},{17,1},{33,17},{49,33},{2,50}... | collective-permute-start | bytes 393224 | tf_op jit(solution)/shard_map/ppermute | solution.py:24
  187.4 18.8 %collective-permute-start.6 = (bf16[128,512]{1,0:T(8,128)(2,1)S(1)}, bf16[128,512]{1,0:T(8,128)(2,1)}, u32[]{:S(2)}, u32[]{:S(2)}) collective-permute-start(bf16[128,512]{1,0:T(8,128)(2,1)S(1)} %get-tuple-element.11), channel_id=1, source_target_pairs={{0,32},{16,48},{32,0},{48,16},{1,33},{17,49},{33,1},{49,17},{2,34}... | collective-permute-start | bytes 393224 | tf_op jit(solution)/shard_map/ppermute | solution.py:24
  207.2 15.1 %collective-permute-start.8 = (bf16[128,512]{1,0:T(8,128)(2,1)S(1)}, bf16[128,512]{1,0:T(8,128)(2,1)S(1)}, u32[]{:S(2)}, u32[]{:S(2)}) collective-permute-start(bf16[128,512]{1,0:T(8,128)(2,1)S(1)} %fusion.24), channel_id=1, source_target_pairs={{0,48},{16,0},{32,16},{48,32},{1,49},{17,1},{33,17},{49,33},{2,50}... | collective-permute-start | bytes 393224 | tf_op jit(solution)/shard_map/ppermute | solution.py:34
  209.0 21.3 %collective-permute-start.10 = (bf16[128,512]{1,0:T(8,128)(2,1)S(1)}, bf16[128,512]{1,0:T(8,128)(2,1)S(1)}, u32[]{:S(2)}, u32[]{:S(2)}) collective-permute-start(bf16[128,512]{1,0:T(8,128)(2,1)S(1)} %fusion.24), channel_id=1, source_target_pairs={{0,16},{16,32},{32,48},{48,0},{1,17},{17,33},{33,49},{49,1},{2,18}... | collective-permute-start | bytes 393224 | tf_op jit(solution)/shard_map/ppermute | solution.py:34
  212.9 17.4 %collective-permute-start.9 = (bf16[128,512]{1,0:T(8,128)(2,1)S(1)}, bf16[128,512]{1,0:T(8,128)(2,1)S(1)}, u32[]{:S(2)}, u32[]{:S(2)}) collective-permute-start(bf16[128,512]{1,0:T(8,128)(2,1)S(1)} %fusion.24), channel_id=1, source_target_pairs={{0,32},{16,48},{32,0},{48,16},{1,33},{17,49},{33,1},{49,17},{2,34}... | collective-permute-start | bytes 393224 | tf_op jit(solution)/shard_map/ppermute | solution.py:34
  230.4 14.0 %collective-permute-start.11 = (bf16[512,512]{1,0:T(8,128)(2,1)S(1)}, bf16[512,512]{1,0:T(8,128)(2,1)S(1)}, u32[]{:S(2)}, u32[]{:S(2)}) collective-permute-start(bf16[512,512]{1,0:T(8,128)(2,1)S(1)} %bitcast.128), channel_id=1, source_target_pairs={{0,192},{64,0},{128,64},{192,128},{1,193},{65,1},{129,65},{193,129... | collective-permute-start | bytes 1572872 | tf_op jit(solution)/shard_map/ppermute | solution.py:34
  231.7 15.7 %collective-permute-start.12 = (bf16[512,512]{1,0:T(8,128)(2,1)S(1)}, bf16[512,512]{1,0:T(8,128)(2,1)}, u32[]{:S(2)}, u32[]{:S(2)}) collective-permute-start(bf16[512,512]{1,0:T(8,128)(2,1)S(1)} %bitcast.129), channel_id=1, source_target_pairs={{0,128},{64,192},{128,0},{192,64},{1,129},{65,193},{129,1},{193,65... | collective-permute-start | bytes 1572872 | tf_op jit(solution)/shard_map/ppermute | solution.py:34
  232.2 26.3 %collective-permute-start.13 = (bf16[512,512]{1,0:T(8,128)(2,1)S(1)}, bf16[512,512]{1,0:T(8,128)(2,1)}, u32[]{:S(2)}, u32[]{:S(2)}) collective-permute-start(bf16[512,512]{1,0:T(8,128)(2,1)S(1)} %bitcast.130), channel_id=1, source_target_pairs={{0,64},{64,128},{128,192},{192,0},{1,65},{65,129},{129,193},{193,1... | collective-permute-start | bytes 1572872 | tf_op jit(solution)/shard_map/ppermute | solution.py:34
  247.1 190.3 %all-reduce.2.cloned.1.call-start = ((), (), s32[]{:S(2)}) async-start(), calls=%async_computation.3 | async-start | bytes 524288 | tf_op jit(solution)/shard_map/psum | solution.py:120
  263.8 14.6 %copy-start.10 = (s32[4096]{0:T(1024)S(1)}, s32[4096]{0:T(1024)}, u32[]{:S(2)}) copy-start(s32[4096]{0:T(1024)} %copy-done.9) | copy-start | bytes 49156
  263.8 14.6 %copy-start.12 = (s32[4096]{0:T(1024)S(1)}, s32[4096]{0:T(1024)}, u32[]{:S(2)}) copy-start(s32[4096]{0:T(1024)} %copy-done.11) | copy-start | bytes 49156
  286.0 4.8 %copy-start.4 = (bf16[1024,4,1,128]{3,0,1,2:T(8,128)(2,1)S(1)}, bf16[1024,4,1,128]{3,0,1,2:T(8,128)(2,1)}, u32[]{:S(2)}) copy-start(bf16[1024,4,1,128]{3,0,1,2:T(8,128)(2,1)} %copy-done.3) | copy-start | bytes 3145732
  286.0 4.8 %copy-start.6 = (bf16[1024,4,1,128]{3,0,1,2:T(8,128)(2,1)S(1)}, bf16[1024,4,1,128]{3,0,1,2:T(8,128)(2,1)}, u32[]{:S(2)}) copy-start(bf16[1024,4,1,128]{3,0,1,2:T(8,128)(2,1)} %copy-done.5) | copy-start | bytes 3145732
  286.8 2.0 copy-start.1
  288.7 6.7 %collective-permute-start.1 = (f32[4,1,128]{2,0,1:T(4,128)S(1)}, f32[4,1,128]{2,0,1:T(4,128)S(1)}, u32[]{:S(2)}, u32[]{:S(2)}) collective-permute-start(f32[4,1,128]{2,0,1:T(4,128)S(1)} %bitcast.152), channel_id=1, source_target_pairs={{0,16},{16,32},{32,48},{1,17},{17,33},{33,49},{2,18},{18,34},{34,5... | collective-permute-start | bytes 6152 | tf_op jit(solution)/shard_map/ppermute | solution.py:13
Sparse Core Ops, SparseCore 0:
  19.7 24.3 all-gather.8
  51.7 78.6 all-gather.4
  147.2 79.1 reduce-scatter.3
  247.2 31.1 all-gather.6
  295.5 141.8 all-reduce.1
